TPU v7x, 32 devices: a whole 2x2x4 slice. The times are simulated.
32 devices in a mesh: group: 2 (over y), seq: 4 (over z), batch: 2 (over x), chan: 2 (over core).
Axes of the slice: x: 2, y: 2, z: 4, core: 2. Of those that a mesh axis runs over, the one named last changes fastest.
Arguments:
- history: bfloat16 [8, 1024, 4096], P(('group', 'batch'), 'seq', 'chan'), parts along dimension 0, may hold values from -6 to 6
- filter_taps: bfloat16 [1024, 4096], P('seq', 'chan'), may hold values from -0.1875 to 0.1875
- lengths: int32 [8], P(('group', 'batch')), parts along dimension 0, may hold values from 256 to 1024, as said below
- inner_gate: bfloat16 [8, 256, 4096], P(('group', 'batch'), 'seq', 'chan'), parts along dimension 0, may hold values from -6 to 6
- values_in: bfloat16 [8, 256, 4096], P(('group', 'batch'), 'seq', 'chan'), parts along dimension 0, may hold values from -6 to 6
- outer_gate: bfloat16 [8, 256, 4096], P(('group', 'batch'), 'seq', 'chan'), parts along dimension 0, may hold values from -6 to 6
- skip_gain: float32 [4096], P('chan'), may hold values from -4 to 4
Outputs:
- mixed: bfloat16 [8, 256, 4096], P(('group', 'batch'), 'seq', 'chan'), parts along dimension 0
- next_history: bfloat16 [8, 1024, 4096], P(('group', 'batch'), 'seq', 'chan'), parts along dimension 0
There are 2 independent parts, one for each index of `group`. A program takes and returns all parts, laid end to end along the dimension named above; an argument that names none is the same for every part. Nothing has to cross between parts.
Inputs may be any that keep to these rules, and one draw needn't show every extreme that they name: `lengths`: each request's prefilled length is a multiple of 256; some request of every part has exactly 1024, and some other is shorter.
All inputs are finite; a program needn't handle non-finite values.
Results may differ from a plain program's by a relative error of at most 0.0044.
Values may be sent and summed in bfloat16 or wider, within the bound.
No kernel may reach another device: no remote copies, remote signals or barrier semaphores. Data moves between devices by JAX's collectives and lax.ppermute only.
A program may use at most 128 MiB of HBM per device.

v0:
```python
import jax
import jax.numpy as jnp
from jax import lax
from jax.sharding import PartitionSpec as P


def from_behind(block, axis, distance):
    devices = range(lax.axis_size(axis))
    route = [(i - distance, i) for i in devices if i - distance in devices]
    return lax.ppermute(block, axis, route)


def correlate(signal, kernel):
    width = signal.shape[2]
    return lax.conv_general_dilated(
        signal,
        kernel[:, None, :],
        (1,),
        "VALID",
        dimension_numbers=("NWC", "WIO", "NWC"),
        feature_group_count=width,
        preferred_element_type=jnp.float32,
    )


def per_device(history, filter_taps, lengths, inner_gate, values_in, outer_gate, skip_gain):
    position = lax.axis_index("seq")
    n_seq = lax.axis_size("seq")
    requests, tile_len, width = history.shape
    own_tokens = inner_gate.shape[1]
    span_len = own_tokens * n_seq
    assert span_len == tile_len
    step = own_tokens
    product_own = (inner_gate.astype(jnp.float32) * values_in.astype(jnp.float32)).astype(
        jnp.bfloat16
    )
    product_all = lax.all_gather(product_own, "seq", axis=1, tiled=True)
    head_product = product_all[:, ::-1]
    row_ids = position * tile_len + jnp.arange(tile_len, dtype=jnp.int32)
    live_rows = jnp.where(
        (row_ids[None, :] < lengths[:, None])[:, :, None], history, jnp.zeros_like(history)
    )
    prev_keep = ((row_ids - tile_len)[None, :] < lengths[:, None])[:, :, None]
    head_parts = []
    prev_live = []
    sums = []
    for c in range(n_seq):
        lo = tile_len - step * (c + 1)
        hi = lo + step
        sent = from_behind(history[:, lo:hi], "seq", 1)
        if c == 0:
            first = product_own[:, ::-1]
        else:
            first = head_product[:, lo:hi]
        head_c = jnp.where(position == 0, first, sent)
        head_parts.append(head_c)
        prev_live.insert(0, jnp.where(prev_keep[:, lo:hi], head_c, jnp.zeros_like(head_c)))
        segment = jnp.concatenate(prev_live + [live_rows[:, : hi - 1]], axis=1)
        partial_rev = correlate(segment, filter_taps)
        sums.append(lax.psum(partial_rev, "seq"))
    own_rev = jnp.stack(sums)[position]
    summed = own_rev[:, ::-1]
    product_float = product_own.astype(jnp.float32)
    total = summed + skip_gain[None, None, :] * product_float
    mixed = (outer_gate.astype(jnp.float32) * total).astype(jnp.bfloat16)
    next_history = jnp.concatenate(head_parts[::-1], axis=1)
    return (mixed, next_history)


def solution(mesh):
    in_specs = (
        P(("group", "batch"), "seq", "chan"),
        P("seq", "chan"),
        P(("group", "batch")),
        P(("group", "batch"), "seq", "chan"),
        P(("group", "batch"), "seq", "chan"),
        P(("group", "batch"), "seq", "chan"),
        P("chan"),
    )
    out_specs = (P(("group", "batch"), "seq", "chan"), P(("group", "batch"), "seq", "chan"))
    return jax.shard_map(
        per_device, mesh=mesh, in_specs=in_specs, out_specs=out_specs, check_vma=False
    )
```

profile of v0, /device:TPU:0, one launch (start us, length us, event | category | flops | bytes accessed | tf_op | source)
XLA Modules:
  0.0 412.6 jit_solution(7550243576826798161)
XLA Ops:
  10.1 2.9 fusion.27
  12.9 5.7 %collective-permute-start = (bf16[2,64,2048]{2,1,0:T(8,128)(2,1)}, bf16[2,64,2048]{2,1,0:T(8,128)(2,1)}, u32[]{:S(2)}, u32[]{:S(2)}) collective-permute-start(bf16[2,64,2048]{2,1,0:T(8,128)(2,1)} %get-tuple-element.21), channel_id=1, source_target_pairs={{0,4},{4,8},{8,12},{1,5},{5,9},{9,13},{2,6},{6,10},{10,14},{3,7},{... | collective-permute-start | bytes 1572872 | tf_op jit(solution)/shard_map/ppermute | solution.py:10
  18.7 3.5 collective-permute-start.1
  22.2 3.5 collective-permute-start.3
  25.7 2.1 collective-permute-start.2
  27.9 1.8 broadcast_select_fusion
  29.8 8.4 %rev.7 = bf16[2,64,2048]{2,1,0:T(8,128)(2,1)} reverse(bf16[2,64,2048]{2,1,0:T(8,128)(2,1)} %copy-done.1), dimensions={1} | reverse | bytes 1048576 | tf_op jit(solution)/shard_map/rev | solution.py:52
  40.6 48.2 %all-gather.2.cloned.1.call-done = bf16[2,256,2048]{2,0,1:T(2,128)(2,1)} async-done(((bf16[2,64,2048]{2,0,1:T(2,128)(2,1)}), bf16[2,256,2048]{2,0,1:T(2,128)(2,1)}) %all-gather.2.cloned.1.call-update) | async-done | bytes 2097168 | tf_op jit(solution)/shard_map/all_gather | solution.py:37
  88.8 3.7 fusion.28
  93.5 8.3 %slice.69 = bf16[2,64,2048]{2,1,0:T(8,128)(2,1)} reverse(bf16[2,64,2048]{2,1,0:T(8,128)(2,1)} %copy.60), dimensions={1} | reverse | bytes 1048576 | tf_op jit(solution)/shard_map/slice | solution.py:54
  101.8 2.2 select_dynamic-update-slice_fusion
  104.0 2.0 copy.59
  106.0 8.3 %slice.64 = bf16[2,64,2048]{2,1,0:T(8,128)(2,1)} reverse(bf16[2,64,2048]{2,1,0:T(8,128)(2,1)} %copy.59), dimensions={1} | reverse | bytes 1048576 | tf_op jit(solution)/shard_map/slice | solution.py:54
  114.3 2.4 constant_dynamic-update-slice_fusion.2
  117.7 8.3 %slice.59 = bf16[2,64,2048]{2,1,0:T(8,128)(2,1)} reverse(bf16[2,64,2048]{2,1,0:T(8,128)(2,1)} %copy.58), dimensions={1} | reverse | bytes 1048576 | tf_op jit(solution)/shard_map/slice | solution.py:54
  126.1 2.3 constant_dynamic-update-slice_fusion.1
  130.5 27.0 %fusion.17 = f32[1,2,64,2048]{3,1,2,0:T(2,128)} fusion(bf16[2,319,2048]{2,1,0:T(8,128)(2,1)} %slice_dynamic-update-slice_fusion, bf16[256,1,2048]{2,0,1:T(8,128)(2,1)S(1)} %bitcast.22), kind=kOutput, calls=%fused_computation.18 | convolution fusion | flops 134217728 | bytes 4710400 | tf_op jit(solution)/shard_map/conv_general_dilated | solution.py:15
  158.6 25.6 %fusion.11 = f32[1,2,64,2048]{3,1,2,0:T(2,128)} fusion(bf16[2,319,2048]{2,1,0:T(8,128)(2,1)S(1)} %get-tuple-element.28, bf16[256,1,2048]{2,0,1:T(8,128)(2,1)S(1)} %bitcast.24), kind=kOutput, calls=%fused_computation.16 | convolution fusion | flops 134217728 | bytes 4710400 | tf_op jit(solution)/shard_map/conv_general_dilated | solution.py:15
  184.2 25.5 %fusion.14 = f32[1,2,64,2048]{3,1,2,0:T(2,128)} fusion(bf16[2,319,2048]{2,1,0:T(8,128)(2,1)S(1)} %get-tuple-element.29, bf16[256,1,2048]{2,0,1:T(8,128)(2,1)S(1)} %bitcast.23), kind=kOutput, calls=%fused_computation.17 | convolution fusion | flops 134217728 | bytes 4710400 | tf_op jit(solution)/shard_map/conv_general_dilated | solution.py:15
  209.7 25.5 %fusion.8 = f32[1,2,64,2048]{3,1,2,0:T(2,128)} fusion(bf16[2,319,2048]{2,1,0:T(8,128)(2,1)S(1)} %get-tuple-element.30, bf16[256,1,2048]{2,0,1:T(8,128)(2,1)S(1)} %bitcast.21), kind=kOutput, calls=%fused_computation.15 | convolution fusion | flops 134217728 | bytes 4710400 | tf_op jit(solution)/shard_map/conv_general_dilated | solution.py:15
  238.2 154.7 %all-reduce.3.cloned.1.call-done = (f32[1,2,64,2048]{3,1,2,0:T(2,128)}, f32[1,2,64,2048]{3,1,2,0:T(2,128)}, f32[1,2,64,2048]{3,1,2,0:T(2,128)}, f32[1,2,64,2048]{3,1,2,0:T(2,128)}) async-done(((f32[1,2,64,2048]{3,1,2,0:T(2,128)}, f32[1,2,64,2048]{3,1,2,0:T(2,128)}, f32[1,2,64,2048]{3,1,2,0:T(2,128)}, f32[1,2,64,2048]{3,1,2,0:T(2,128)}), (f32[1,2,64,2048]{3,1,2,0:T(2,128)}, f32[1,2,64,2048]{3,1,2,0:T(2,128)}, ...) | async-done | bytes 4194320 | tf_op jit(solution)/shard_map/psum | solution.py:60
  392.9 3.3 fusion.22
  396.3 1.6 copy.86
  397.9 6.8 %rev.8 = f32[2,64,2048]{2,1,0:T(8,128)S(1)} reverse(f32[2,64,2048]{2,1,0:T(8,128)} %bitcast.26), dimensions={1} | reverse | bytes 2097152 | tf_op jit(solution)/shard_map/rev | solution.py:62
  (53 shorter events, 14.7 us)
Async XLA Ops:
  7.2 123.4 %copy-start = (bf16[256,2048]{1,0:T(8,128)(2,1)S(1)}, bf16[256,2048]{1,0:T(8,128)(2,1)}, u32[]{:S(2)}) copy-start(bf16[256,2048]{1,0:T(8,128)(2,1)} %param.8) | copy-start | bytes 3145732
  7.2 81.6 %all-gather.2.cloned.1.call-start = ((), (), s32[]{:S(2)}) async-start(), calls=%async_computation | async-start | bytes 2621440 | tf_op jit(solution)/shard_map/all_gather | solution.py:37
  8.6 19.2 %copy-start.1 = (bf16[2,64,2048]{2,1,0:T(8,128)(2,1)}, bf16[2,64,2048]{2,1,0:T(8,128)(2,1)S(1)}, u32[]{:S(2)}) copy-start(bf16[2,64,2048]{2,1,0:T(8,128)(2,1)S(1)} %multiply_convert_fusion.1) | copy-start | bytes 1572868
  10.0 17.8 %copy-start.14 = (s32[2]{0:T(128)S(1)}, s32[2]{0:T(128)}, u32[]{:S(2)}) copy-start(s32[2]{0:T(128)} %param.9) | copy-start | bytes 28
  10.0 382.9 %all-reduce.3.cloned.1.call-start = ((), (), s32[]{:S(2)}) async-start(), calls=%async_computation.1 | async-start | bytes 8388608 | tf_op jit(solution)/shard_map/psum | solution.py:60
  12.9 115.5 %collective-permute-start = (bf16[2,64,2048]{2,1,0:T(8,128)(2,1)}, bf16[2,64,2048]{2,1,0:T(8,128)(2,1)}, u32[]{:S(2)}, u32[]{:S(2)}) collective-permute-start(bf16[2,64,2048]{2,1,0:T(8,128)(2,1)} %get-tuple-element.21), channel_id=1, source_target_pairs={{0,4},{4,8},{8,12},{1,5},{5,9},{9,13},{2,6},{6,10},{10,14},{3,7},{... | collective-permute-start | bytes 1572872 | tf_op jit(solution)/shard_map/ppermute | solution.py:10
  18.7 107.4 %collective-permute-start.1 = (bf16[2,64,2048]{2,1,0:T(8,128)(2,1)}, bf16[2,64,2048]{2,1,0:T(8,128)(2,1)}, u32[]{:S(2)}, u32[]{:S(2)}) collective-permute-start(bf16[2,64,2048]{2,1,0:T(8,128)(2,1)} %get-tuple-element.22), channel_id=1, source_target_pairs={{0,4},{4,8},{8,12},{1,5},{5,9},{9,13},{2,6},{6,10},{10,14},{3,7},{... | collective-permute-start | bytes 1572872 | tf_op jit(solution)/shard_map/ppermute | solution.py:10
  22.2 79.6 %collective-permute-start.3 = (bf16[2,64,2048]{2,1,0:T(8,128)(2,1)}, bf16[2,64,2048]{2,1,0:T(8,128)(2,1)}, u32[]{:S(2)}, u32[]{:S(2)}) collective-permute-start(bf16[2,64,2048]{2,1,0:T(8,128)(2,1)} %get-tuple-element.23), channel_id=1, source_target_pairs={{0,4},{4,8},{8,12},{1,5},{5,9},{9,13},{2,6},{6,10},{10,14},{3,7},{... | collective-permute-start | bytes 1572872 | tf_op jit(solution)/shard_map/ppermute | solution.py:10
  25.7 88.7 %collective-permute-start.2 = (bf16[2,64,2048]{2,1,0:T(8,128)(2,1)}, bf16[2,64,2048]{2,1,0:T(8,128)(2,1)}, u32[]{:S(2)}, u32[]{:S(2)}) collective-permute-start(bf16[2,64,2048]{2,1,0:T(8,128)(2,1)} %get-tuple-element.24), channel_id=1, source_target_pairs={{0,4},{4,8},{8,12},{1,5},{5,9},{9,13},{2,6},{6,10},{10,14},{3,7},{... | collective-permute-start | bytes 1572872 | tf_op jit(solution)/shard_map/ppermute | solution.py:10
  114.3 2.5 copy-start.7
  126.1 2.3 copy-start.6
  130.5 27.0 %copy-start.3 = (bf16[2,191,2048]{2,1,0:T(8,128)(2,1)S(1)}, bf16[2,191,2048]{2,1,0:T(8,128)(2,1)}, u32[]{:S(2)}) copy-start(bf16[2,191,2048]{2,1,0:T(8,128)(2,1)} %slice.76) | copy-start | bytes 4694020
  130.5 27.0 %copy-start.4 = (bf16[2,127,2048]{2,1,0:T(8,128)(2,1)S(1)}, bf16[2,127,2048]{2,1,0:T(8,128)(2,1)}, u32[]{:S(2)}) copy-start(bf16[2,127,2048]{2,1,0:T(8,128)(2,1)} %slice.79) | copy-start | bytes 3121156
  130.5 27.0 %copy-start.5 = (bf16[2,64,2048]{2,1,0:T(8,128)(2,1)S(1)}, bf16[2,64,2048]{2,1,0:T(8,128)(2,1)}, u32[]{:S(2)}) copy-start(bf16[2,64,2048]{2,1,0:T(8,128)(2,1)} %get-tuple-element.17) | copy-start | bytes 1572868
  235.1 1.0 copy-start.8
  235.1 1.2 copy-start.9
  235.1 1.4 copy-start.10
  235.1 1.5 copy-start.11
  396.3 8.5 %copy-start.2 = (bf16[2,64,2048]{2,1,0:T(8,128)(2,1)S(1)}, bf16[2,64,2048]{2,1,0:T(8,128)(2,1)}, u32[]{:S(2)}) copy-start(bf16[2,64,2048]{2,1,0:T(8,128)(2,1)} %copy-done.1) | copy-start | bytes 1572868
  396.3 8.5 %copy-start.12 = (bf16[2,64,2048]{2,1,0:T(8,128)(2,1)S(1)}, bf16[2,64,2048]{2,1,0:T(8,128)(2,1)}, u32[]{:S(2)}) copy-start(bf16[2,64,2048]{2,1,0:T(8,128)(2,1)} %param.12) | copy-start | bytes 1572868
  396.3 8.5 %copy-start.13 = (f32[2048]{0:T(1024)S(1)}, f32[2048]{0:T(1024)}, u32[]{:S(2)}) copy-start(f32[2048]{0:T(1024)} %param.13) | copy-start | bytes 24580
Sparse Core Ops, SparseCore 0:
  10.2 78.5 all-gather.1
  235.3 157.6 all-reduce.2
where the time goes:
time: 417 us; the launch traced here: 413 us
  waiting for transfers between devices  203 us (49%)
  matrix products  103 us (25%)
  local copies, waits for them, and re-layouts  58.5 us (14%)
  other arithmetic  18.6 us (4%)
  starting transfers between devices  14.9 us (4%)
  between operations  14.2 us (3%)
    psum x1, waiting for transfers between devices, per_device(): sums.append(lax.psum(partial_rev, 'seq'))  155 us
    conv_general_dilated x4, matrix products, correlate(): lax.conv_general_dilated(signal, kernel[:, None, :], (1,), 'VALID', dimen...  103 us
    all_gather x1, waiting for transfers between devices, per_device(): product_all = lax.all_gather(product_own, 'seq', axis=1, tiled=True)  48.2 us
    slice x4, local copies, waits for them, and re-layouts, per_device(): first = head_product[:, lo:hi]  28.7 us
    ppermute x4, starting transfers between devices, from_behind(): return lax.ppermute(block, axis, route)  14.8 us
    rev x1, local copies, waits for them, and re-layouts, per_device(): first = product_own[:, ::-1]  8.36 us
  transfers between devices with their start and end apart: 6, of which 2 were waited for; matrix products, arithmetic and copies ran while one was open for 14% of the time, Pallas kernels for 0%

commit v1 on v0

--- a/solution.py
+++ b/solution.py
@@ -57,7 +57,7 @@
         prev_live.insert(0, jnp.where(prev_keep[:, lo:hi], head_c, jnp.zeros_like(head_c)))
         segment = jnp.concatenate(prev_live + [live_rows[:, : hi - 1]], axis=1)
         partial_rev = correlate(segment, filter_taps)
-        sums.append(lax.psum(partial_rev, "seq"))
+        sums.append(jnp.sum(lax.all_gather(partial_rev, "seq"), axis=0))
     own_rev = jnp.stack(sums)[position]
     summed = own_rev[:, ::-1]
     product_float = product_own.astype(jnp.float32)

time: 417 us -> 509 us (1.22)
  waiting for transfers between devices: 203 us -> 279 us
  other arithmetic: 18.6 us -> 33.5 us
    all_gather x0 -> x4, waiting for transfers between devices: none -> 227 us  [per_device(): sums.append(jnp.sum(lax.all_gather(partial_rev, 'seq'), axis=0))]
    psum x1 -> x0, waiting for transfers between devices: 155 us -> none  [per_device(): sums.append(lax.psum(partial_rev, 'seq'))]
    reduce_sum x0 -> x4, other arithmetic: none -> 13.7 us  [per_device(): sums.append(jnp.sum(lax.all_gather(partial_rev, 'seq'), axis=0))]
    conv_general_dilated x0 -> x4, local copies, waits for them, and re-layouts: none -> 6.36 us  [correlate(): lax.conv_general_dilated(signal, kernel[:, None, :], (1,), 'VALID', dimen...]
  transfers between devices with their start and end apart: 6 -> 9, of which waited for: 2 -> 4; matrix products, arithmetic and copies ran while one was open for 14% -> 29% of each run, Pallas kernels for 0% -> 0%
where the time goes in v1:
time: 509 us; the launch traced here: 505 us
  waiting for transfers between devices  279 us (55%)
  matrix products  104 us (20%)
  local copies, waits for them, and re-layouts  59.9 us (12%)
  other arithmetic  33.5 us (7%)
  starting transfers between devices  15.2 us (3%)
  between operations  14 us (3%)
    all_gather x4, waiting for transfers between devices, per_device(): sums.append(jnp.sum(lax.all_gather(partial_rev, 'seq'), axis=0))  227 us
    conv_general_dilated x4, matrix products, correlate(): lax.conv_general_dilated(signal, kernel[:, None, :], (1,), 'VALID', dimen...  104 us
    all_gather x1, waiting for transfers between devices, per_device(): product_all = lax.all_gather(product_own, 'seq', axis=1, tiled=True)  52.1 us
    slice x4, local copies, waits for them, and re-layouts, per_device(): first = head_product[:, lo:hi]  28.6 us
    ppermute x4, starting transfers between devices, from_behind(): return lax.ppermute(block, axis, route)  14.8 us
    reduce_sum x4, other arithmetic, per_device(): sums.append(jnp.sum(lax.all_gather(partial_rev, 'seq'), axis=0))  13.7 us
  transfers between devices with their start and end apart: 9, of which 4 were waited for; matrix products, arithmetic and copies ran while one was open for 29% of the time, Pallas kernels for 0%

profile of v1, /device:TPU:0, one launch (start us, length us, event | category | flops | bytes accessed | tf_op | source)
XLA Modules:
  0.0 504.9 jit_solution(5615697466927409385)
XLA Ops:
  12.4 5.7 %collective-permute-start = (bf16[2,64,2048]{2,1,0:T(8,128)(2,1)}, bf16[2,64,2048]{2,1,0:T(8,128)(2,1)}, u32[]{:S(2)}, u32[]{:S(2)}) collective-permute-start(bf16[2,64,2048]{2,1,0:T(8,128)(2,1)} %get-tuple-element.19), channel_id=1, source_target_pairs={{0,4},{4,8},{8,12},{1,5},{5,9},{9,13},{2,6},{6,10},{10,14},{3,7},{... | collective-permute-start | bytes 1572872 | tf_op jit(solution)/shard_map/ppermute | solution.py:10
  18.1 3.5 collective-permute-start.1
  21.6 3.5 collective-permute-start.3
  29.2 8.3 %rev.7 = bf16[2,64,2048]{2,1,0:T(8,128)(2,1)} reverse(bf16[2,64,2048]{2,1,0:T(8,128)(2,1)} %copy-done.1), dimensions={1} | reverse | bytes 1048576 | tf_op jit(solution)/shard_map/rev | solution.py:52
  37.5 52.1 %all-gather.10.cloned.1.call-done = bf16[2,256,2048]{2,0,1:T(2,128)(2,1)} async-done(((bf16[2,64,2048]{2,0,1:T(2,128)(2,1)}), bf16[2,256,2048]{2,0,1:T(2,128)(2,1)}) %all-gather.10.cloned.1.call-update) | async-done | bytes 2097168 | tf_op jit(solution)/shard_map/all_gather | solution.py:37
  89.6 3.6 fusion.17
  94.2 8.3 %slice.69 = bf16[2,64,2048]{2,1,0:T(8,128)(2,1)} reverse(bf16[2,64,2048]{2,1,0:T(8,128)(2,1)} %copy.90), dimensions={1} | reverse | bytes 1048576 | tf_op jit(solution)/shard_map/slice | solution.py:54
  106.8 8.3 %slice.64 = bf16[2,64,2048]{2,1,0:T(8,128)(2,1)} reverse(bf16[2,64,2048]{2,1,0:T(8,128)(2,1)} %copy.89), dimensions={1} | reverse | bytes 1048576 | tf_op jit(solution)/shard_map/slice | solution.py:54
  115.1 2.5 constant_dynamic-update-slice_fusion.2
  118.5 8.3 %slice.59 = bf16[2,64,2048]{2,1,0:T(8,128)(2,1)} reverse(bf16[2,64,2048]{2,1,0:T(8,128)(2,1)} %copy.88), dimensions={1} | reverse | bytes 1048576 | tf_op jit(solution)/shard_map/slice | solution.py:54
  131.5 26.2 %fusion = f32[2,64,2048]{2,0,1:T(2,128)S(1)} fusion(bf16[2,319,2048]{2,1,0:T(8,128)(2,1)} %slice_dynamic-update-slice_fusion, bf16[256,1,2048]{2,0,1:T(8,128)(2,1)S(1)} %bitcast.21), kind=kOutput, calls=%fused_computation.7 | convolution fusion | flops 134217728 | bytes 4710400 | tf_op jit(solution)/shard_map/conv_general_dilated | solution.py:15
  160.8 2.7 pad_maximum_fusion.2
  163.5 24.9 %fusion.2 = f32[2,64,2048]{2,0,1:T(2,128)S(1)} fusion(bf16[2,319,2048]{2,1,0:T(8,128)(2,1)S(1)} %get-tuple-element.26, bf16[256,1,2048]{2,0,1:T(8,128)(2,1)S(1)} %bitcast.22), kind=kOutput, calls=%fused_computation.9 | convolution fusion | flops 134217728 | bytes 4710400 | tf_op jit(solution)/shard_map/conv_general_dilated | solution.py:15
  190.0 26.2 %fusion.4 = f32[2,64,2048]{2,0,1:T(2,128)S(1)} fusion(bf16[2,319,2048]{2,1,0:T(8,128)(2,1)} %get-tuple-element.27, bf16[256,1,2048]{2,0,1:T(8,128)(2,1)S(1)} %bitcast.23), kind=kOutput, calls=%fused_computation.11 | convolution fusion | flops 134217728 | bytes 4710400 | tf_op jit(solution)/shard_map/conv_general_dilated | solution.py:15
  218.2 26.2 %fusion.6 = f32[2,64,2048]{2,0,1:T(2,128)S(1)} fusion(bf16[2,319,2048]{2,1,0:T(8,128)(2,1)} %get-tuple-element.28, bf16[256,1,2048]{2,0,1:T(8,128)(2,1)S(1)} %bitcast.20), kind=kOutput, calls=%fused_computation.13 | convolution fusion | flops 134217728 | bytes 4710400 | tf_op jit(solution)/shard_map/conv_general_dilated | solution.py:15
  247.5 3.0 reduce_sum.39
  250.6 72.2 %all-gather.16.cloned.1.call-done = f32[8,64,2048]{2,1,0:T(8,128)} async-done(((f32[2,64,2048]{2,1,0:T(8,128)}), f32[8,64,2048]{2,1,0:T(8,128)}) %all-gather.16.cloned.1.call-update) | async-done | bytes 4194320 | tf_op jit(solution)/shard_map/all_gather | solution.py:60
  322.8 3.6 reduce_sum.38
  326.3 77.2 %all-gather.14.cloned.1.call-done = f32[8,64,2048]{2,1,0:T(8,128)} async-done(((f32[2,64,2048]{2,1,0:T(8,128)}), f32[8,64,2048]{2,1,0:T(8,128)}) %all-gather.14.cloned.1.call-update) | async-done | bytes 4194320 | tf_op jit(solution)/shard_map/all_gather | solution.py:60
  403.5 3.6 reduce_sum.37
  407.1 77.2 %all-gather.12.cloned.1.call-done = f32[8,64,2048]{2,1,0:T(8,128)} async-done(((f32[2,64,2048]{2,1,0:T(8,128)}), f32[8,64,2048]{2,1,0:T(8,128)}) %all-gather.12.cloned.1.call-update) | async-done | bytes 4194320 | tf_op jit(solution)/shard_map/all_gather | solution.py:60
  484.3 3.6 reduce_sum.36
  487.8 2.6 fusion.11
  490.5 6.8 %rev.8 = f32[2,64,2048]{2,1,0:T(8,128)S(1)} reverse(f32[2,64,2048]{2,1,0:T(8,128)} %fusion.11), dimensions={1} | reverse | bytes 2097152 | tf_op jit(solution)/shard_map/rev | solution.py:62
  (71 shorter events, 30.6 us)
Async XLA Ops:
  7.2 124.3 %copy-start = (bf16[256,2048]{1,0:T(8,128)(2,1)S(1)}, bf16[256,2048]{1,0:T(8,128)(2,1)}, u32[]{:S(2)}) copy-start(bf16[256,2048]{1,0:T(8,128)(2,1)} %param.8) | copy-start | bytes 3145732
  7.2 3.8 copy-start.3
  7.2 82.4 %all-gather.10.cloned.1.call-start = ((), (), s32[]{:S(2)}) async-start(), calls=%async_computation | async-start | bytes 2621440 | tf_op jit(solution)/shard_map/all_gather | solution.py:37
  10.9 16.3 %copy-start.15 = (s32[2]{0:T(128)S(1)}, s32[2]{0:T(128)}, u32[]{:S(2)}) copy-start(s32[2]{0:T(128)} %param.9) | copy-start | bytes 28
  10.9 236.7 %all-gather.18.cloned.1.call-start = ((), (), s32[]{:S(2)}) async-start(), calls=%async_computation.4 | async-start | bytes 5242880 | tf_op jit(solution)/shard_map/all_gather | solution.py:60
  12.4 116.9 %collective-permute-start = (bf16[2,64,2048]{2,1,0:T(8,128)(2,1)}, bf16[2,64,2048]{2,1,0:T(8,128)(2,1)}, u32[]{:S(2)}, u32[]{:S(2)}) collective-permute-start(bf16[2,64,2048]{2,1,0:T(8,128)(2,1)} %get-tuple-element.19), channel_id=1, source_target_pairs={{0,4},{4,8},{8,12},{1,5},{5,9},{9,13},{2,6},{6,10},{10,14},{3,7},{... | collective-permute-start | bytes 1572872 | tf_op jit(solution)/shard_map/ppermute | solution.py:10
  18.1 108.8 %collective-permute-start.1 = (bf16[2,64,2048]{2,1,0:T(8,128)(2,1)}, bf16[2,64,2048]{2,1,0:T(8,128)(2,1)}, u32[]{:S(2)}, u32[]{:S(2)}) collective-permute-start(bf16[2,64,2048]{2,1,0:T(8,128)(2,1)} %get-tuple-element.20), channel_id=1, source_target_pairs={{0,4},{4,8},{8,12},{1,5},{5,9},{9,13},{2,6},{6,10},{10,14},{3,7},{... | collective-permute-start | bytes 1572872 | tf_op jit(solution)/shard_map/ppermute | solution.py:10
  21.6 81.0 %collective-permute-start.3 = (bf16[2,64,2048]{2,1,0:T(8,128)(2,1)}, bf16[2,64,2048]{2,1,0:T(8,128)(2,1)}, u32[]{:S(2)}, u32[]{:S(2)}) collective-permute-start(bf16[2,64,2048]{2,1,0:T(8,128)(2,1)} %get-tuple-element.21), channel_id=1, source_target_pairs={{0,4},{4,8},{8,12},{1,5},{5,9},{9,13},{2,6},{6,10},{10,14},{3,7},{... | collective-permute-start | bytes 1572872 | tf_op jit(solution)/shard_map/ppermute | solution.py:10
  25.1 90.0 %collective-permute-start.2 = (bf16[2,64,2048]{2,1,0:T(8,128)(2,1)}, bf16[2,64,2048]{2,1,0:T(8,128)(2,1)}, u32[]{:S(2)}, u32[]{:S(2)}) collective-permute-start(bf16[2,64,2048]{2,1,0:T(8,128)(2,1)} %get-tuple-element.22), channel_id=1, source_target_pairs={{0,4},{4,8},{8,12},{1,5},{5,9},{9,13},{2,6},{6,10},{10,14},{3,7},{... | collective-permute-start | bytes 1572872 | tf_op jit(solution)/shard_map/ppermute | solution.py:10
  115.1 2.5 copy-start.8
  126.8 2.4 copy-start.7
  159.3 163.4 %all-gather.16.cloned.1.call-start = ((), (), s32[]{:S(2)}) async-start(), calls=%async_computation.3 | async-start | bytes 5242880 | tf_op jit(solution)/shard_map/all_gather | solution.py:60
  159.4 1.0 copy-start.4
  159.4 1.2 copy-start.5
  159.4 1.3 copy-start.6
  190.0 213.5 %all-gather.14.cloned.1.call-start = ((), (), s32[]{:S(2)}) async-start(), calls=%async_computation.2 | async-start | bytes 5242880 | tf_op jit(solution)/shard_map/all_gather | solution.py:60
  217.9 266.3 %all-gather.12.cloned.1.call-start = ((), (), s32[]{:S(2)}) async-start(), calls=%async_computation.1 | async-start | bytes 5242880 | tf_op jit(solution)/shard_map/all_gather | solution.py:60
  244.4 1.7 copy-start.9
  244.4 1.7 copy-start.10
  244.4 1.7 copy-start.11
  244.4 1.7 copy-start.12
  487.8 9.5 %copy-start.2 = (bf16[2,64,2048]{2,1,0:T(8,128)(2,1)S(1)}, bf16[2,64,2048]{2,1,0:T(8,128)(2,1)}, u32[]{:S(2)}) copy-start(bf16[2,64,2048]{2,1,0:T(8,128)(2,1)} %copy-done.1) | copy-start | bytes 1572868
  487.8 9.5 %copy-start.13 = (bf16[2,64,2048]{2,1,0:T(8,128)(2,1)S(1)}, bf16[2,64,2048]{2,1,0:T(8,128)(2,1)}, u32[]{:S(2)}) copy-start(bf16[2,64,2048]{2,1,0:T(8,128)(2,1)} %param.12) | copy-start | bytes 1572868
  487.8 9.5 %copy-start.14 = (f32[2048]{0:T(1024)S(1)}, f32[2048]{0:T(1024)}, u32[]{:S(2)}) copy-start(f32[2048]{0:T(1024)} %param.13) | copy-start | bytes 24580
  (1 other events, 0.8 us)
Sparse Core Ops, SparseCore 0:
  11.0 78.5 all-gather.9
  159.5 82.3 all-gather.17
  243.4 79.2 all-gather.15
  324.2 79.2 all-gather.13
  404.9 79.2 all-gather.11
